TPU v7x, 32 devices: a whole 2x2x4 slice. The times are simulated.
32 devices in a mesh: seq: 4 (over y, x), exp: 8 (over z, core).
Axes of the slice: x: 2, y: 2, z: 4, core: 2. Of those that a mesh axis runs over, the one named last changes fastest.
Arguments:
- token_ids: int32 [4, 32], replicated, may hold values from 0 to 51199
- cache_lengths: int32 [32], replicated, may hold values from 1 to 1024, as said below
- empty_blocks: int32 [32, 64], replicated, may hold values 0 or 1
- expert_ids: int32 [4, 32, 6], replicated, may hold values from 0 to 63, all different within a row
- embed_table: bfloat16 [51200, 2048], P(('seq', 'exp')), may hold values from -3 to 3
- attn_gain: float32 [2048], replicated, may hold values from 0.5 to 1.5
- w_query: bfloat16 [2048, 2048], P(None, 'seq'), may hold values from -0.125 to 0.125
- w_key: bfloat16 [2048, 2048], P(None, 'seq'), may hold values from -0.125 to 0.125
- w_value: bfloat16 [2048, 2048], P(None, 'seq'), may hold values from -0.125 to 0.125
- w_out: bfloat16 [2048, 2048], P('seq'), may hold values from -0.125 to 0.125
- k_cache: bfloat16 [32, 1024, 2048], P('exp', 'seq'), may hold values from -200 to 200
- v_cache: bfloat16 [32, 1024, 2048], P('exp', 'seq'), may hold values from -6 to 6
- moe_gain: float32 [2048], replicated, may hold values from 0.5 to 1.5
- w_router: bfloat16 [2048, 64], replicated, may hold values from -0.125 to 0.125
- gate_pieces: bfloat16 [256, 2048, 352], P(('seq', 'exp')), may hold values from -0.125 to 0.125
- up_pieces: bfloat16 [256, 2048, 352], P(('seq', 'exp')), may hold values from -0.125 to 0.125
- down_pieces: bfloat16 [256, 352, 2048], P(('seq', 'exp')), may hold values from -0.15625 to 0.15625
- shared_gate: bfloat16 [2048, 2816], P(None, 'exp'), may hold values from -0.125 to 0.125
- shared_up: bfloat16 [2048, 2816], P(None, 'exp'), may hold values from -0.125 to 0.125
- shared_down: bfloat16 [2816, 2048], P('exp'), may hold values from -0.109375 to 0.109375
- final_gain: float32 [2048], replicated, may hold values from 0.5 to 1.5
- w_head: bfloat16 [2048, 51200], P(None, ('seq', 'exp')), may hold values from -0.125 to 0.125
Outputs:
- hidden_norms: float32 [4, 32], replicated
- greatest_logits: float32 [4, 32], replicated
Inputs may be any that keep to these rules, and one draw needn't show every extreme that they name: `cache_lengths`: one of the 32 requests has exactly 1024 cached positions in every draw.
All inputs are finite; a program needn't handle non-finite values.
Results may differ from a plain program's by a relative error of at most 0.0055.
Values may be sent and summed in bfloat16 or wider, within the bound.
No kernel may reach another device: no remote copies, remote signals or barrier semaphores. Data moves between devices by JAX's collectives and lax.ppermute only.
A program may use at most 128 MiB of HBM per device.

v0:
```python
import math
import jax
import jax.numpy as jnp
from jax import lax
from jax.sharding import PartitionSpec as P

HDIM = 128
PIECES = 4
BLK = 16
epsilon = 1e-06
negative = -1e30


def rms_scale(values, scales):
    return values * lax.rsqrt(jnp.mean(values * values, axis=-1, keepdims=True) + epsilon) * scales


def rotate(values, places):
    half_width = values.shape[-1] // 2
    frequency = 10000.0 ** (-2.0 * jnp.arange(half_width, dtype=jnp.float32) / values.shape[-1])
    angles = places.astype(jnp.float32)[..., None, None] * frequency
    cosine_table = jnp.cos(angles)
    sine_table = jnp.sin(angles)
    lower = values[..., :half_width]
    upper = values[..., half_width:]
    return jnp.concatenate(
        [lower * cosine_table - upper * sine_table, upper * cosine_table + lower * sine_table],
        axis=-1,
    )


def gather_all(values):
    inner = lax.all_gather(values, "exp", axis=0, tiled=False)
    return lax.all_gather(inner, "seq", axis=0, tiled=False)


def on_device(
    token_ids,
    cache_lengths,
    empty_blocks,
    expert_ids,
    embed_table,
    attn_gain,
    w_query,
    w_key,
    w_value,
    w_out,
    k_cache,
    v_cache,
    moe_gain,
    w_router,
    gate_pieces,
    up_pieces,
    down_pieces,
    shared_gate,
    shared_up,
    shared_down,
    final_gain,
    w_head,
):
    steps, requests = token_ids.shape
    tokens = steps * requests
    width = embed_table.shape[1]
    vocab_local = embed_table.shape[0]
    n_seq = lax.axis_size("seq")
    n_exp = lax.axis_size("exp")
    n_dev = n_seq * n_exp
    owner_index = lax.axis_index(("seq", "exp"))
    seq_index = lax.axis_index("seq")
    own_count = requests // n_exp
    own_start = lax.axis_index("exp") * own_count
    group = steps * own_count
    share = group // n_seq

    def permuted(values):
        rest = values.shape[2:]
        grouped = jnp.moveaxis(values.reshape((steps, n_exp, own_count) + rest), 1, 0)
        split = grouped.reshape((n_exp, n_seq, share) + rest)
        return jnp.swapaxes(split, 0, 1).reshape((tokens,) + rest)

    def natural(values):
        split = jnp.swapaxes(values.reshape(n_seq, n_exp, share), 0, 1)
        grouped = split.reshape(n_exp, steps, own_count)
        return jnp.moveaxis(grouped, 0, 1).reshape(steps, requests)

    local_ids = token_ids - owner_index * vocab_local
    held = (local_ids >= 0) & (local_ids < vocab_local)
    rows = jnp.take(embed_table, jnp.clip(local_ids, 0, vocab_local - 1), axis=0)
    rows = jnp.where(held[..., None], rows, jnp.zeros((), rows.dtype))
    rows = jnp.moveaxis(rows.reshape(steps, n_exp, own_count, width), 1, 0)
    arrived = lax.all_to_all(rows, "exp", 0, 0, tiled=True)
    row_part = jnp.sum(arrived.astype(jnp.float32), axis=0).astype(jnp.bfloat16)
    row_parts = lax.all_gather(row_part, "seq", axis=0, tiled=False)
    embedded = jnp.sum(row_parts.astype(jnp.float32), axis=0).reshape(group, width)
    attn_in = rms_scale(embedded, attn_gain).astype(jnp.bfloat16)
    own_lengths = lax.dynamic_slice_in_dim(cache_lengths, own_start, own_count, 0)
    places = (own_lengths[None, :] + jnp.arange(steps, dtype=jnp.int32)[:, None]).reshape(group)
    heads_here = w_query.shape[1] // HDIM

    def project(weight):
        return jnp.dot(attn_in, weight, preferred_element_type=jnp.float32).reshape(
            group, heads_here, HDIM
        )

    query_part = rotate(project(w_query), places).astype(jnp.bfloat16)
    key_part = rotate(project(w_key), places).astype(jnp.bfloat16)
    value_part = project(w_value).astype(jnp.bfloat16)
    every = lax.all_gather(
        jnp.stack([query_part, key_part, value_part], axis=0), "seq", axis=0, tiled=False
    )
    head_count = n_seq * heads_here
    every = jnp.moveaxis(every, 0, 2).reshape(3, steps, own_count, head_count, HDIM)
    queries = every[0]
    span = k_cache.shape[1]
    first_place = seq_index * span
    places_here = first_place + jnp.arange(span, dtype=jnp.int32)
    own_empty = lax.dynamic_slice_in_dim(empty_blocks, own_start, own_count, 0)
    local_blocks = lax.dynamic_slice_in_dim(own_empty, first_place // BLK, span // BLK, 1)
    blocked = jnp.broadcast_to(local_blocks[:, :, None], (own_count, span // BLK, BLK)).reshape(
        own_count, span
    )
    live_mask = ((places_here[None, :] < own_lengths[:, None]) & (blocked == 0))[None, :, None, :]
    cache_keys = k_cache.reshape(own_count, span, head_count, HDIM)
    cache_values = v_cache.reshape(own_count, span, head_count, HDIM)
    score_scale = 1.0 / math.sqrt(HDIM)
    cached = (
        jnp.einsum("trhd,rphd->trhp", queries, cache_keys, preferred_element_type=jnp.float32)
        * score_scale
    )
    local_top = jnp.max(jnp.where(live_mask, cached, negative), axis=3)
    local_weights = jnp.where(live_mask, jnp.exp(cached - local_top[..., None]), 0.0)
    local_totals = jnp.sum(local_weights, axis=3)
    local_mixture = jnp.einsum(
        "trhp,rphd->trhd",
        local_weights.astype(jnp.bfloat16),
        cache_values,
        preferred_element_type=jnp.float32,
    )

    def by_owner(values):
        rest = values.shape[3:]
        split = values.reshape((steps, own_count, n_seq, heads_here) + rest)
        return jnp.moveaxis(split, 2, 0).reshape(n_seq, -1)

    mix_len = group * heads_here * HDIM
    stat_len = group * heads_here
    packed = jnp.concatenate(
        [by_owner(local_mixture), by_owner(local_top), by_owner(local_totals)], axis=1
    )
    got = lax.all_to_all(packed, "seq", 0, 0, tiled=True)
    got_mixture = got[:, :mix_len].reshape(n_seq, steps, own_count, heads_here, HDIM)
    got_top = got[:, mix_len : mix_len + stat_len].reshape(n_seq, steps, own_count, heads_here)
    got_totals = got[:, mix_len + stat_len :].reshape(n_seq, steps, own_count, heads_here)
    own_queries = query_part.reshape(steps, own_count, heads_here, HDIM)
    own_keys = key_part.reshape(steps, own_count, heads_here, HDIM)
    own_values = value_part.reshape(steps, own_count, heads_here, HDIM)
    fresh_scores = (
        jnp.einsum("trhd,urhd->trhu", own_queries, own_keys, preferred_element_type=jnp.float32)
        * score_scale
    )
    causal = (jnp.arange(steps)[None, :] <= jnp.arange(steps)[:, None])[:, None, None, :]
    fresh_top = jnp.max(jnp.where(causal, fresh_scores, negative), axis=3)
    fresh_weights = jnp.where(causal, jnp.exp(fresh_scores - fresh_top[..., None]), 0.0)
    fresh_mixture = jnp.einsum(
        "trhu,urhd->trhd",
        fresh_weights.astype(jnp.bfloat16),
        own_values,
        preferred_element_type=jnp.float32,
    )
    top_score = jnp.maximum(jnp.max(got_top, axis=0), fresh_top)
    cache_factor = jnp.exp(got_top - top_score[None])
    fresh_factor = jnp.exp(fresh_top - top_score)
    totals = (
        jnp.sum(got_totals * cache_factor, axis=0) + jnp.sum(fresh_weights, axis=3) * fresh_factor
    )
    mixture = (
        jnp.sum(got_mixture * cache_factor[..., None], axis=0)
        + fresh_mixture * fresh_factor[..., None]
    )
    own_heads = (mixture / totals[..., None]).astype(jnp.bfloat16).reshape(group, heads_here * HDIM)
    attn_part = jnp.dot(own_heads, w_out, preferred_element_type=jnp.float32)
    attn_sum = jnp.sum(
        lax.all_to_all(attn_part.reshape(n_seq, share, width), "seq", 0, 0, tiled=True), axis=0
    )
    resid_share = lax.dynamic_slice_in_dim(embedded, seq_index * share, share, 0) + attn_sum
    moe_in = gather_all(rms_scale(resid_share, moe_gain).astype(jnp.bfloat16)).reshape(
        tokens, width
    )
    router = jax.nn.sigmoid(jnp.dot(moe_in, w_router, preferred_element_type=jnp.float32))
    expert_count = w_router.shape[1]
    chosen_ids = permuted(expert_ids)
    picked = chosen_ids[:, :, None] == jnp.arange(expert_count, dtype=jnp.int32)[None, None, :]
    chosen = jnp.sum(jnp.where(picked, router[:, None, :], 0.0), axis=2)
    gate_weights = chosen / jnp.sum(chosen, axis=1, keepdims=True)
    rows_here = gate_pieces.shape[0]
    row_expert = (owner_index * rows_here + jnp.arange(rows_here, dtype=jnp.int32)) // PIECES
    token_weight = jnp.sum(
        jnp.where(
            chosen_ids[None, :, :] == row_expert[:, None, None], gate_weights[None, :, :], 0.0
        ),
        axis=2,
    )
    gate_out = jnp.einsum("nd,jdf->jnf", moe_in, gate_pieces, preferred_element_type=jnp.float32)
    up_out = jnp.einsum("nd,jdf->jnf", moe_in, up_pieces, preferred_element_type=jnp.float32)
    expert_hidden = (jax.nn.silu(gate_out) * up_out).astype(jnp.bfloat16)
    expert_out = jnp.einsum(
        "jnf,jfd->jnd", expert_hidden, down_pieces, preferred_element_type=jnp.float32
    )
    routed = jnp.einsum("jn,jnd->nd", token_weight, expert_out)
    share_count = tokens // n_seq
    share_start = seq_index * share_count
    share_rows = lax.dynamic_slice_in_dim(moe_in, share_start, share_count, 0)
    shared_hidden = (
        jax.nn.silu(jnp.dot(share_rows, shared_gate, preferred_element_type=jnp.float32))
        * jnp.dot(share_rows, shared_up, preferred_element_type=jnp.float32)
    ).astype(jnp.bfloat16)
    shared_out = jnp.dot(shared_hidden, shared_down, preferred_element_type=jnp.float32)
    term_rows = lax.dynamic_update_slice_in_dim(
        routed,
        lax.dynamic_slice_in_dim(routed, share_start, share_count, 0) + shared_out,
        share_start,
        0,
    )
    term_sum = jnp.sum(
        lax.all_to_all(term_rows.reshape(n_dev, share, width), ("seq", "exp"), 0, 0, tiled=True),
        axis=0,
    )
    final_share = resid_share + term_sum
    norms_share = jnp.sqrt(jnp.mean(final_share * final_share, axis=-1))
    head_in = gather_all(rms_scale(final_share, final_gain).astype(jnp.bfloat16)).reshape(
        tokens, width
    )
    local_best = jnp.max(jnp.dot(head_in, w_head, preferred_element_type=jnp.float32), axis=-1)
    message = jnp.concatenate([local_best, norms_share], axis=0)
    heard = lax.all_to_all(
        jnp.broadcast_to(message[None, :], (n_dev, message.shape[0])),
        ("seq", "exp"),
        0,
        0,
        tiled=True,
    )
    greatest_logits = natural(jnp.max(heard[:, :tokens], axis=0))
    hidden_norms = natural(heard[:, tokens:].reshape(tokens))
    return (hidden_norms, greatest_logits)


def solution(mesh):
    in_specs = (
        P(),
        P(),
        P(),
        P(),
        P(("seq", "exp"), None),
        P(),
        P(None, "seq"),
        P(None, "seq"),
        P(None, "seq"),
        P("seq", None),
        P("exp", "seq", None),
        P("exp", "seq", None),
        P(),
        P(),
        P(("seq", "exp"), None, None),
        P(("seq", "exp"), None, None),
        P(("seq", "exp"), None, None),
        P(None, "exp"),
        P(None, "exp"),
        P("exp", None),
        P(),
        P(None, ("seq", "exp")),
    )
    out_specs = (P(), P())
    return jax.shard_map(
        on_device, mesh=mesh, in_specs=in_specs, out_specs=out_specs, check_vma=False
    )
```

profile of v0, /device:TPU:0, one launch (start us, length us, event | category | flops | bytes accessed | tf_op | source)
XLA Modules:
  0.0 212.5 jit_solution(10068466699584656610)
XLA Ops:
  0.7 0.8 compare_and_fusion.1
  1.6 5.1 %gather_fusion = bf16[128,2048]{1,0:T(8,128)(2,1)S(1)} fusion(bf16[1600,2048]{1,0:T(8,128)(2,1)} %param.26, s32[1024]{0:T(1024)S(1)} %pad_clamp_fusion), kind=kCustom, calls=%fused_computation | custom fusion | bytes 1049088 | tf_op jit(solution)/shard_map/jit(_take)/gather | solution.py:88
  7.2 1.2 fusion.31
  8.4 6.3 %all-to-all-start = ((bf16[8,4,4,2048]{3,2,1,0:T(4,128)(2,1)}), bf16[8,4,4,2048]{3,2,1,0:T(4,128)(2,1)S(1)}, u32[]{:S(2)}, u32[]{:S(2)}) async-start(bf16[8,4,4,2048]{3,2,1,0:T(4,128)(2,1)} %fusion.31), calls=%async_computation | async-start | bytes 1048576 | tf_op jit(solution)/shard_map/all_to_all | solution.py:91
  14.8 4.0 %copy.152 = bf16[512,2048]{1,0:T(8,128)(2,1)} copy(bf16[512,2048]{0,1:T(8,128)(2,1)} %bitcast.138) | data formatting | bytes 4194304 | tf_op jit(solution)/shard_map/dot_general | solution.py:101
  18.8 3.9 %copy.153 = bf16[512,2048]{1,0:T(8,128)(2,1)} copy(bf16[512,2048]{0,1:T(8,128)(2,1)} %bitcast.139) | data formatting | bytes 4194304 | tf_op jit(solution)/shard_map/dot_general | solution.py:101
  22.8 4.0 %copy.154 = bf16[512,2048]{1,0:T(8,128)(2,1)} copy(bf16[512,2048]{0,1:T(8,128)(2,1)} %bitcast.140) | data formatting | bytes 4194304 | tf_op jit(solution)/shard_map/dot_general | solution.py:101
  28.1 2.0 all-to-all-done
  30.3 9.0 %all-gather = bf16[16,4,2048]{2,1,0:T(4,128)(2,1)S(1)} all-gather(bf16[4,4,2048]{2,1,0:T(4,128)(2,1)S(1)} %reduce_sum.137), channel_id=2, replica_groups=mesh['seq'=4,'exp'=8] {'seq'}, dimensions={0}, use_global_device_ids=true | all-gather | bytes 327680 | tf_op jit(solution)/shard_map/all_gather | solution.py:93
  39.7 2.4 %fusion.74 = f32[16,4,128]{2,0,1:T(8,128)S(1)} fusion(bf16[16,2048,1]{1,0,2:T(8,128)(2,1)S(1)} %reshape.564, bf16[4,128,2048]{2,1,0:T(8,128)(2,1)} %bitcast.136), kind=kOutput, calls=%fused_computation.132 | convolution fusion | flops 33554432 | bytes 2195456 | tf_op jit(solution)/shard_map/dot_general | solution.py:101
  43.4 2.2 %convolution_convert_fusion = bf16[16,4,128]{2,0,1:T(8,128)(2,1)S(1)} fusion(bf16[16,2048,1]{1,0,2:T(8,128)(2,1)S(1)} %reshape.564, bf16[4,128,2048]{2,1,0:T(8,128)(2,1)} %bitcast.134), kind=kOutput, calls=%fused_computation.34 | convolution fusion | flops 33562624 | bytes 2179072 | tf_op jit(solution)/shard_map/dot_general | solution.py:101
  45.7 8.8 %all-gather.1 = bf16[12,16,4,128]{3,1,2,0:T(8,128)(2,1)S(1)} all-gather(bf16[3,16,4,128]{3,1,2,0:T(8,128)(2,1)S(1)} %pad_maximum_fusion), channel_id=3, replica_groups=mesh['seq'=4,'exp'=8] {'seq'}, dimensions={0}, use_global_device_ids=true | all-gather | bytes 245760 | tf_op jit(solution)/shard_map/all_gather | solution.py:108
  54.7 3.5 %select_reduce_fusion = (f32[4,4,16]{0,2,1:T(8,128)S(1)}, f32[4,4,16,256]{3,0,2,1:T(4,128)S(1)}) fusion(pred[4,256]{1,0:T(4,128)(4,1)S(1)} %compare_and_fusion, bf16[4,4,16,128]{3,2,1,0:T(8,128)(2,1)S(1)} %bitcast.167, bf16[4,256,2048]{2,1,0:T(8,128)(2,1)} %param.32), kind=kOutput, calls=%fused_computation.42 | convolution fusion | flops 16973568 | bytes 4524032 | tf_op jit(solution)/shard_map/trhd,rphd->trhp/dot_general | solution.py:127
  58.7 2.9 %fusion.2 = f32[4,16,4,128]{3,2,1,0:T(4,128)S(1)} fusion(f32[4,4,16,256]{3,0,2,1:T(4,128)S(1)} %get-tuple-element.27, f32[4,4,16]{0,2,1:T(8,128)S(1)} %get-tuple-element.26, pred[4,256]{1,0:T(4,128)(4,1)S(1)} %compare_and_fusion, bf16[4,256,2048]{2,1,0:T(8,128)(2,1)} %param.33), kind=kOutput, calls=%fused_computation.3 | convolution fusion | flops 16973824 | bytes 4589568 | tf_op jit(solution)/shard_map/trhp,rphd->trhd/dot_general | solution.py:133
  62.2 0.8 copy.135
  63.0 3.3 %all-to-all-start.1 = ((f32[4,1,8320]{2,1,0:T(1,128)}), f32[4,1,8320]{2,1,0:T(1,128)S(1)}, u32[]{:S(2)}, u32[]{:S(2)}) async-start(f32[4,1,8320]{2,1,0:T(1,128)} %copy.135), calls=%async_computation.1 | async-start | bytes 266240 | tf_op jit(solution)/shard_map/all_to_all | solution.py:150
  66.4 4.9 %all-to-all-done.1 = f32[4,1,8320]{2,1,0:T(1,128)S(1)} async-done(((f32[4,1,8320]{2,1,0:T(1,128)}), f32[4,1,8320]{2,1,0:T(1,128)S(1)}, u32[]{:S(2)}, u32[]{:S(2)}) %all-to-all-start.1) | async-done | bytes 133152 | tf_op jit(solution)/shard_map/all_to_all | solution.py:150
  72.8 1.0 fusion.9
  73.8 3.5 %all-to-all-start.2 = ((f32[4,4,2048]{2,1,0:T(4,128)}), f32[4,4,2048]{2,1,0:T(4,128)S(1)}, u32[]{:S(2)}, u32[]{:S(2)}) async-start(f32[4,4,2048]{2,1,0:T(4,128)} %fusion.9), calls=%async_computation.2 | async-start | bytes 262144 | tf_op jit(solution)/shard_map/all_to_all | solution.py:183
  77.4 4.9 %all-to-all-done.2 = f32[4,4,2048]{2,1,0:T(4,128)S(1)} async-done(((f32[4,4,2048]{2,1,0:T(4,128)}), f32[4,4,2048]{2,1,0:T(4,128)S(1)}, u32[]{:S(2)}, u32[]{:S(2)}) %all-to-all-start.2) | async-done | bytes 131104 | tf_op jit(solution)/shard_map/all_to_all | solution.py:183
  82.5 14.0 %all-gather.6 = bf16[8,4,2048]{2,1,0:T(4,128)(2,1)S(1)} all-gather(bf16[1,4,2048]{2,1,0:T(4,128)(2,1)S(1)} %fusion.53), channel_id=4, replica_groups=mesh['seq'=4,'exp'=8] {'exp'}, dimensions={0}, use_global_device_ids=true | all-gather | bytes 147456 | tf_op jit(solution)/shard_map/all_gather | solution.py:33
  96.5 9.8 %all-gather.3 = bf16[32,4,2048]{2,1,0:T(4,128)(2,1)S(1)} all-gather(bf16[8,4,2048]{2,1,0:T(4,128)(2,1)S(1)} %all-gather.6), channel_id=5, replica_groups=mesh['seq'=4,'exp'=8] {'seq'}, dimensions={0}, use_global_device_ids=true | all-gather | bytes 655360 | tf_op jit(solution)/shard_map/all_gather | solution.py:34
  107.1 6.2 %convolution_bitcast_fusion.1 = f32[8,128,352]{1,2,0:T(8,128)S(1)} fusion(bf16[128,2048,1]{1,0,2:T(8,128)(2,1)S(1)} %reshape.566, bf16[8,2048,352]{1,2,0:T(8,128)(2,1)} %param.36), kind=kOutput, calls=%fused_computation.14 | convolution fusion | flops 1476395008 | bytes 13500416 | tf_op jit(solution)/shard_map/nd,jdf->jnf/dot_general | solution.py:203
  113.4 18.6 %fusion.13 = bf16[8,128,2048]{2,1,0:T(8,128)(2,1)} fusion(bf16[8,352,2048]{2,1,0:T(8,128)(2,1)} %param.38, bf16[128,2048,1]{1,0,2:T(8,128)(2,1)S(1)} %reshape.566, bf16[8,2048,352]{1,2,0:T(8,128)(2,1)} %param.37, f32[8,128,352]{1,2,0:T(8,128)S(1)} %convolution_bitcast_fusion.1), kind=kOutput, calls=%fused_computation.17 | convolution fusion | flops 2954952704 | bytes 29229056 | tf_op jit(solution)/shard_map/jnf,jfd->jnd/dot_general | solution.py:206
  132.0 5.3 %fusion = f32[128,1,2048]{2,1,0:T(1,128)S(1)} fusion(bf16[8,128,1]{0,2,1:T(2,128)(2,1)S(1)} %copy.149, bf16[8,128,2048]{2,1,0:T(8,128)(2,1)} %fusion.13), kind=kOutput, calls=%fused_computation.1 | convolution fusion | flops 4194304 | bytes 5244928 | tf_op jit(solution)/shard_map/jn,jnd->nd/dot_general | solution.py:209
  137.7 1.0 copy-done.3
  139.2 3.2 %fusion.8 = f32[128,2048]{1,0:T(8,128)S(1)} fusion(f32[128,2048]{1,0:T(8,128)S(1)} %bitcast.137, s32[]{:T(128)S(6)} %select_n.86, bf16[352,2048]{1,0:T(8,128)(2,1)} %param.41, bf16[2048,352]{0,1:T(8,128)(2,1)} %param.40, bf16[128,2048]{1,0:T(8,128)(2,1)S(1)} %reshape.535, f32[32,352]{1,0:T(8,128)S(1)} %fusion.41), kind=kOutput, calls=%fused_computation.10 | convolution fusion | flops 92407808 | bytes 3589120 | tf_op jit(solution)/shard_map/dot_general | solution.py:217
  142.7 30.4 %all_to_all.36 = f32[32,4,2048]{2,1,0:T(4,128)S(1)} all-to-all(f32[32,4,2048]{2,1,0:T(4,128)S(1)} %reshape.536), channel_id=1, replica_groups=mesh['seq'=4,'exp'=8] {'seq','exp'}, dimensions={0} | all-to-all | bytes 2097152 | tf_op jit(solution)/shard_map/all_to_all | solution.py:225
  173.5 14.0 %all-gather.7 = bf16[8,4,2048]{2,1,0:T(4,128)(2,1)S(1)} all-gather(bf16[1,4,2048]{2,1,0:T(4,128)(2,1)S(1)} %fusion.54), channel_id=6, replica_groups=mesh['seq'=4,'exp'=8] {'exp'}, dimensions={0}, use_global_device_ids=true | all-gather | bytes 147456 | tf_op jit(solution)/shard_map/all_gather | solution.py:33
  187.4 9.4 %all-gather.5 = bf16[32,4,2048]{2,1,0:T(4,128)(2,1)S(1)} all-gather(bf16[8,4,2048]{2,1,0:T(4,128)(2,1)S(1)} %all-gather.7), channel_id=7, replica_groups=mesh['seq'=4,'exp'=8] {'seq'}, dimensions={0}, use_global_device_ids=true | all-gather | bytes 655360 | tf_op jit(solution)/shard_map/all_gather | solution.py:34
  196.9 4.9 %convolution_reduce_fusion = f32[128]{0:T(128)S(1)} fusion(bf16[128,2048]{1,0:T(8,128)(2,1)S(1)} %reshape.537, bf16[2048,1600]{0,1:T(8,128)(2,1)} %param.43), kind=kOutput, calls=%fused_computation.18 | convolution fusion | flops 839065472 | bytes 7078400 | tf_op jit(solution)/shard_map/dot_general | solution.py:233
  201.9 9.3 %all_to_all.37 = f32[32,1,132]{2,1,0:T(1,128)S(1)} all-to-all(f32[32,1,132]{2,1,0:T(1,128)S(1)} %broadcast_in_dim.150), channel_id=1, replica_groups=mesh['seq'=4,'exp'=8] {'seq','exp'}, dimensions={0} | all-to-all | bytes 33792 | tf_op jit(solution)/shard_map/all_to_all | solution.py:235
  (111 shorter events, 10.7 us)
Async XLA Ops:
  0.6 72.1 %copy-start = (bf16[512,2048]{1,0:T(8,128)(2,1)S(1)}, bf16[512,2048]{1,0:T(8,128)(2,1)}, u32[]{:S(2)}) copy-start(bf16[512,2048]{1,0:T(8,128)(2,1)} %param.31) | copy-start | bytes 6291460
  6.7 8.0 %copy-start.9 = (s32[32]{0:T(128)S(1)}, s32[32]{0:T(128)}, u32[]{:S(2)}) copy-start(s32[32]{0:T(128)} %param.23) | copy-start | bytes 388
  8.4 21.7 %all-to-all-start = ((bf16[8,4,4,2048]{3,2,1,0:T(4,128)(2,1)}), bf16[8,4,4,2048]{3,2,1,0:T(4,128)(2,1)S(1)}, u32[]{:S(2)}, u32[]{:S(2)}) async-start(bf16[8,4,4,2048]{3,2,1,0:T(4,128)(2,1)} %fusion.31), calls=%async_computation | async-start | bytes 1048576 | tf_op jit(solution)/shard_map/all_to_all | solution.py:91
  22.8 5.0 %copy-start.5 = (s32[4,32,6]{1,0,2:T(4,128)S(1)}, s32[4,32,6]{1,0,2:T(4,128)}, u32[]{:S(2)}) copy-start(s32[4,32,6]{1,0,2:T(4,128)} %param.25) | copy-start | bytes 9220
  22.8 16.8 %copy-start.6 = (f32[2048]{0:T(1024)S(1)}, f32[2048]{0:T(1024)}, u32[]{:S(2)}) copy-start(f32[2048]{0:T(1024)} %param.27) | copy-start | bytes 24580
  39.7 2.4 %copy-start.2 = (bf16[512,2048]{1,0:T(8,128)(2,1)S(1)}, bf16[512,2048]{1,0:T(8,128)(2,1)}, u32[]{:S(2)}) copy-start(bf16[512,2048]{1,0:T(8,128)(2,1)} %copy.153) | copy-start | bytes 6291460
  63.0 8.3 %all-to-all-start.1 = ((f32[4,1,8320]{2,1,0:T(1,128)}), f32[4,1,8320]{2,1,0:T(1,128)S(1)}, u32[]{:S(2)}, u32[]{:S(2)}) async-start(f32[4,1,8320]{2,1,0:T(1,128)} %copy.135), calls=%async_computation.1 | async-start | bytes 266240 | tf_op jit(solution)/shard_map/all_to_all | solution.py:150
  72.3 10.1 %copy-start.7 = (f32[2048]{0:T(1024)S(1)}, f32[2048]{0:T(1024)}, u32[]{:S(2)}) copy-start(f32[2048]{0:T(1024)} %param.34) | copy-start | bytes 24580
  73.8 32.7 %copy-start.4 = (bf16[2048,64]{0,1:T(8,128)(2,1)S(1)}, bf16[2048,64]{0,1:T(8,128)(2,1)}, u32[]{:S(2)}) copy-start(bf16[2048,64]{0,1:T(8,128)(2,1)} %param.35) | copy-start | bytes 786436
  73.8 8.4 %all-to-all-start.2 = ((f32[4,4,2048]{2,1,0:T(4,128)}), f32[4,4,2048]{2,1,0:T(4,128)S(1)}, u32[]{:S(2)}, u32[]{:S(2)}) async-start(f32[4,4,2048]{2,1,0:T(4,128)} %fusion.9), calls=%async_computation.2 | async-start | bytes 262144 | tf_op jit(solution)/shard_map/all_to_all | solution.py:183
  137.3 1.4 copy-start.3
  142.7 30.7 %copy-start.8 = (f32[2048]{0:T(1024)S(1)}, f32[2048]{0:T(1024)}, u32[]{:S(2)}) copy-start(f32[2048]{0:T(1024)} %param.42) | copy-start | bytes 24580
  196.9 15.6 %copy-start.1 = (bf16[512,2048]{1,0:T(8,128)(2,1)S(1)}, bf16[512,2048]{1,0:T(8,128)(2,1)}, u32[]{:S(2)}) copy-start(bf16[512,2048]{1,0:T(8,128)(2,1)} %param.31) | copy-start | bytes 6291460
where the time goes:
time: 214 us; the launch traced here: 213 us
  blocking collectives  105 us (49%)
  matrix products  52.2 us (24%)
  local copies, waits for them, and re-layouts  24.4 us (11%)
  starting transfers between devices  13.1 us (6%)
  waiting for transfers between devices  11.9 us (6%)
  other arithmetic  5.27 us (2%)
    all_to_all x1, blocking collectives, on_device(): lax.all_to_all(term_rows.reshape(n_dev, share, width), ('seq', 'exp'), 0,...  30.4 us
    all_gather x2, blocking collectives, gather_all(): inner = lax.all_gather(values, 'exp', axis=0, tiled=False)  27.9 us
    all_gather x2, blocking collectives, gather_all(): return lax.all_gather(inner, 'seq', axis=0, tiled=False)  19.1 us
    dot_general x1, matrix products, on_device(): jnp.einsum('jnf,jfd->jnd', expert_hidden, down_pieces, preferred_element_...  18.6 us
    dot_general x3, local copies, waits for them, and re-layouts, project(): jnp.dot(attn_in, weight, preferred_element_type=jnp.float32)  11.9 us
    all_to_all x1, blocking collectives, on_device(): lax.all_to_all(jnp.broadcast_to(message[None, :], (n_dev, message.shape[0...  9.33 us
    all_gather x1, blocking collectives, on_device(): row_parts = lax.all_gather(row_part, 'seq', axis=0, tiled=False)  9 us
    all_gather x1, blocking collectives, on_device(): lax.all_gather(jnp.stack([query_part, key_part, value_part], axis=0), 'se...  8.83 us
  transfers between devices with their start and end apart: 3, of which 3 were waited for; matrix products, arithmetic and copies ran while one was open for 6% of the time, Pallas kernels for 0%

commit v1 on v0

--- a/solution.py
+++ b/solution.py
@@ -9,6 +9,28 @@
 BLK = 16
 epsilon = 1e-06
 negative = -1e30
+
+
+def split_up(x, dim, size):
+    before, after = (x.shape[:dim], x.shape[dim + 1 :])
+    return jnp.moveaxis(x.reshape(*before, size, -1, *after), dim, 0)
+
+
+def in_order(blocks, dim):
+    shape = list(blocks.shape[1:])
+    shape[dim] *= blocks.shape[0]
+    return jnp.moveaxis(blocks, 0, dim).reshape(shape)
+
+
+def exchange_in_pairs(value, axis, split_dim, concat_dim):
+    peers, index = (lax.axis_size(axis), lax.axis_index(axis))
+    parts = split_up(value, split_dim, peers)
+    gathered = [parts[index]]
+    for step in range(1, peers):
+        sent = parts[index ^ step]
+        gathered.append(lax.ppermute(sent, axis, [(i, i ^ step) for i in range(peers)]))
+    parts = jnp.stack(gathered)[index ^ jnp.arange(peers)]
+    return in_order(parts, concat_dim)
 
 
 def rms_scale(values, scales):
@@ -147,7 +169,7 @@
     packed = jnp.concatenate(
         [by_owner(local_mixture), by_owner(local_top), by_owner(local_totals)], axis=1
     )
-    got = lax.all_to_all(packed, "seq", 0, 0, tiled=True)
+    got = exchange_in_pairs(packed, "seq", 0, 0)
     got_mixture = got[:, :mix_len].reshape(n_seq, steps, own_count, heads_here, HDIM)
     got_top = got[:, mix_len : mix_len + stat_len].reshape(n_seq, steps, own_count, heads_here)
     got_totals = got[:, mix_len + stat_len :].reshape(n_seq, steps, own_count, heads_here)

time: 214 us -> 210 us (0.981)
  waiting for transfers between devices: 11.9 us -> 9.75 us
    all_to_all x1 -> x0, waiting for transfers between devices: 4.95 us -> none  [on_device(): got = lax.all_to_all(packed, 'seq', 0, 0, tiled=True)]
    ppermute x0 -> x3, starting transfers between devices: none -> 3.55 us  [exchange_in_pairs(): lax.ppermute(sent, axis, [(i, i ^ step) for i in range(peers)])]
    all_to_all x1 -> x0, starting transfers between devices: 3.32 us -> none  [on_device(): got = lax.all_to_all(packed, 'seq', 0, 0, tiled=True)]
    ppermute x0 -> x3, waiting for transfers between devices: none -> 2.86 us  [exchange_in_pairs(): lax.ppermute(sent, axis, [(i, i ^ step) for i in range(peers)])]
  transfers between devices with their start and end apart: 3 -> 5, of which waited for: 3 -> 4; matrix products, arithmetic and copies ran while one was open for 6% -> 7% of each run, Pallas kernels for 0% -> 0%
where the time goes in v1:
time: 210 us; the launch traced here: 209 us
  blocking collectives  105 us (50%)
  matrix products  50.6 us (24%)
  local copies, waits for them, and re-layouts  24.3 us (12%)
  starting transfers between devices  13.3 us (6%)
  waiting for transfers between devices  9.75 us (5%)
  other arithmetic  5.42 us (3%)
    all_to_all x1, blocking collectives, on_device(): lax.all_to_all(term_rows.reshape(n_dev, share, width), ('seq', 'exp'), 0,...  30.4 us
    all_gather x2, blocking collectives, gather_all(): inner = lax.all_gather(values, 'exp', axis=0, tiled=False)  27.9 us
    all_gather x2, blocking collectives, gather_all(): return lax.all_gather(inner, 'seq', axis=0, tiled=False)  19.1 us
    dot_general x1, matrix products, on_device(): jnp.einsum('jnf,jfd->jnd', expert_hidden, down_pieces, preferred_element_...  18.6 us
    dot_general x3, local copies, waits for them, and re-layouts, project(): jnp.dot(attn_in, weight, preferred_element_type=jnp.float32)  11.9 us
    all_to_all x1, blocking collectives, on_device(): lax.all_to_all(jnp.broadcast_to(message[None, :], (n_dev, message.shape[0...  9.33 us
    all_gather x1, blocking collectives, on_device(): row_parts = lax.all_gather(row_part, 'seq', axis=0, tiled=False)  9 us
    all_gather x1, blocking collectives, on_device(): lax.all_gather(jnp.stack([query_part, key_part, value_part], axis=0), 'se...  8.83 us
  transfers between devices with their start and end apart: 5, of which 4 were waited for; matrix products, arithmetic and copies ran while one was open for 7% of the time, Pallas kernels for 0%

profile of v1, /device:TPU:0, one launch (start us, length us, event | category | flops | bytes accessed | tf_op | source)
XLA Modules:
  0.0 209.2 jit_solution(15471977043995112771)
XLA Ops:
  0.7 0.8 compare_and_fusion.1
  1.6 5.1 %gather_fusion = bf16[128,2048]{1,0:T(8,128)(2,1)S(1)} fusion(bf16[1600,2048]{1,0:T(8,128)(2,1)} %param.26, s32[1024]{0:T(1024)S(1)} %pad_clamp_fusion.1), kind=kCustom, calls=%fused_computation | custom fusion | bytes 1049088 | tf_op jit(solution)/shard_map/jit(_take)/gather | solution.py:110
  7.2 1.2 fusion.31
  8.4 6.3 %all-to-all-start = ((bf16[8,4,4,2048]{3,2,1,0:T(4,128)(2,1)}), bf16[8,4,4,2048]{3,2,1,0:T(4,128)(2,1)S(1)}, u32[]{:S(2)}, u32[]{:S(2)}) async-start(bf16[8,4,4,2048]{3,2,1,0:T(4,128)(2,1)} %fusion.31), calls=%async_computation | async-start | bytes 1048576 | tf_op jit(solution)/shard_map/all_to_all | solution.py:113
  14.8 0.8 dynamic-slice_compare_fusion
  15.6 4.0 %copy.150 = bf16[512,2048]{1,0:T(8,128)(2,1)} copy(bf16[512,2048]{0,1:T(8,128)(2,1)} %bitcast.143) | data formatting | bytes 4194304 | tf_op jit(solution)/shard_map/dot_general | solution.py:123
  19.6 3.9 %copy.151 = bf16[512,2048]{1,0:T(8,128)(2,1)} copy(bf16[512,2048]{0,1:T(8,128)(2,1)} %bitcast.144) | data formatting | bytes 4194304 | tf_op jit(solution)/shard_map/dot_general | solution.py:123
  23.6 4.0 %copy.152 = bf16[512,2048]{1,0:T(8,128)(2,1)} copy(bf16[512,2048]{0,1:T(8,128)(2,1)} %bitcast.145) | data formatting | bytes 4194304 | tf_op jit(solution)/shard_map/dot_general | solution.py:123
  28.1 2.0 all-to-all-done
  30.3 9.0 %all-gather = bf16[16,4,2048]{2,1,0:T(4,128)(2,1)S(1)} all-gather(bf16[4,4,2048]{2,1,0:T(4,128)(2,1)S(1)} %reduce_sum.137), channel_id=2, replica_groups=mesh['seq'=4,'exp'=8] {'seq'}, dimensions={0}, use_global_device_ids=true | all-gather | bytes 327680 | tf_op jit(solution)/shard_map/all_gather | solution.py:115
  39.7 2.4 %fusion.75 = f32[16,4,128]{2,0,1:T(8,128)S(1)} fusion(bf16[16,2048,1]{1,0,2:T(8,128)(2,1)S(1)} %reshape.601, bf16[4,128,2048]{2,1,0:T(8,128)(2,1)} %bitcast.141), kind=kOutput, calls=%fused_computation.140 | convolution fusion | flops 33554432 | bytes 2195456 | tf_op jit(solution)/shard_map/dot_general | solution.py:123
  43.7 8.8 %all-gather.1 = bf16[12,16,4,128]{3,1,2,0:T(8,128)(2,1)S(1)} all-gather(bf16[3,16,4,128]{3,1,2,0:T(8,128)(2,1)S(1)} %pad_maximum_fusion), channel_id=3, replica_groups=mesh['seq'=4,'exp'=8] {'seq'}, dimensions={0}, use_global_device_ids=true | all-gather | bytes 245760 | tf_op jit(solution)/shard_map/all_gather | solution.py:130
  52.7 3.5 %select_reduce_fusion = (f32[4,4,16]{0,2,1:T(8,128)S(1)}, f32[4,4,16,256]{3,0,2,1:T(4,128)S(1)}) fusion(pred[4,256]{1,0:T(4,128)(4,1)S(1)} %compare_and_fusion, bf16[4,4,16,128]{3,2,1,0:T(8,128)(2,1)S(1)} %bitcast.168, bf16[4,256,2048]{2,1,0:T(8,128)(2,1)} %param.32), kind=kOutput, calls=%fused_computation.43 | convolution fusion | flops 16973568 | bytes 4524032 | tf_op jit(solution)/shard_map/trhd,rphd->trhp/dot_general | solution.py:149
  56.7 2.9 %fusion.2 = f32[4,16,4,128]{3,2,1,0:T(4,128)S(1)} fusion(f32[4,4,16,256]{3,0,2,1:T(4,128)S(1)} %get-tuple-element.31, f32[4,4,16]{0,2,1:T(8,128)S(1)} %get-tuple-element.30, pred[4,256]{1,0:T(4,128)(4,1)S(1)} %compare_and_fusion, bf16[4,256,2048]{2,1,0:T(8,128)(2,1)} %param.33), kind=kOutput, calls=%fused_computation.4 | convolution fusion | flops 16973824 | bytes 4589568 | tf_op jit(solution)/shard_map/trhp,rphd->trhd/dot_general | solution.py:155
  60.8 1.6 collective-permute-start.1
  62.4 1.5 collective-permute-start.2
  64.7 2.5 %collective-permute-done.2 = f32[1,8320]{1,0:T(1,128)S(1)} collective-permute-done((f32[1,8320]{1,0:T(1,128)S(1)}, f32[1,8320]{1,0:T(1,128)S(1)}, u32[]{:S(2)}, u32[]{:S(2)}) %collective-permute-start.2) | collective-permute-done | bytes 33312 | tf_op jit(solution)/shard_map/ppermute | solution.py:31
  69.4 1.0 fusion.9
  70.5 3.5 %all-to-all-start.1 = ((f32[4,4,2048]{2,1,0:T(4,128)}), f32[4,4,2048]{2,1,0:T(4,128)S(1)}, u32[]{:S(2)}, u32[]{:S(2)}) async-start(f32[4,4,2048]{2,1,0:T(4,128)} %fusion.9), calls=%async_computation.1 | async-start | bytes 262144 | tf_op jit(solution)/shard_map/all_to_all | solution.py:205
  74.0 4.9 %all-to-all-done.1 = f32[4,4,2048]{2,1,0:T(4,128)S(1)} async-done(((f32[4,4,2048]{2,1,0:T(4,128)}), f32[4,4,2048]{2,1,0:T(4,128)S(1)}, u32[]{:S(2)}, u32[]{:S(2)}) %all-to-all-start.1) | async-done | bytes 131104 | tf_op jit(solution)/shard_map/all_to_all | solution.py:205
  79.2 14.0 %all-gather.6 = bf16[8,4,2048]{2,1,0:T(4,128)(2,1)S(1)} all-gather(bf16[1,4,2048]{2,1,0:T(4,128)(2,1)S(1)} %fusion.53), channel_id=4, replica_groups=mesh['seq'=4,'exp'=8] {'exp'}, dimensions={0}, use_global_device_ids=true | all-gather | bytes 147456 | tf_op jit(solution)/shard_map/all_gather | solution.py:55
  93.1 9.8 %all-gather.3 = bf16[32,4,2048]{2,1,0:T(4,128)(2,1)S(1)} all-gather(bf16[8,4,2048]{2,1,0:T(4,128)(2,1)S(1)} %all-gather.6), channel_id=5, replica_groups=mesh['seq'=4,'exp'=8] {'seq'}, dimensions={0}, use_global_device_ids=true | all-gather | bytes 655360 | tf_op jit(solution)/shard_map/all_gather | solution.py:56
  103.8 6.2 %convolution_bitcast_fusion.1 = f32[8,128,352]{1,2,0:T(8,128)S(1)} fusion(bf16[128,2048,1]{1,0,2:T(8,128)(2,1)S(1)} %reshape.603, bf16[8,2048,352]{1,2,0:T(8,128)(2,1)} %param.36), kind=kOutput, calls=%fused_computation.15 | convolution fusion | flops 1476395008 | bytes 13500416 | tf_op jit(solution)/shard_map/nd,jdf->jnf/dot_general | solution.py:225
  110.0 18.6 %fusion.13 = bf16[8,128,2048]{2,1,0:T(8,128)(2,1)} fusion(bf16[8,352,2048]{2,1,0:T(8,128)(2,1)} %param.38, bf16[128,2048,1]{1,0,2:T(8,128)(2,1)S(1)} %reshape.603, bf16[8,2048,352]{1,2,0:T(8,128)(2,1)} %param.37, f32[8,128,352]{1,2,0:T(8,128)S(1)} %convolution_bitcast_fusion.1), kind=kOutput, calls=%fused_computation.18 | convolution fusion | flops 2954952704 | bytes 29229056 | tf_op jit(solution)/shard_map/jnf,jfd->jnd/dot_general | solution.py:228
  128.6 5.3 %fusion = f32[128,1,2048]{2,1,0:T(1,128)S(1)} fusion(bf16[8,128,1]{0,2,1:T(2,128)(2,1)S(1)} %copy.147, bf16[8,128,2048]{2,1,0:T(8,128)(2,1)} %fusion.13), kind=kOutput, calls=%fused_computation.2 | convolution fusion | flops 4194304 | bytes 5244928 | tf_op jit(solution)/shard_map/jn,jnd->nd/dot_general | solution.py:231
  134.3 1.0 copy-done.4
  135.8 3.2 %fusion.8 = f32[128,2048]{1,0:T(8,128)S(1)} fusion(f32[128,2048]{1,0:T(8,128)S(1)} %bitcast.142, s32[]{:T(128)S(6)} %select_n.113, bf16[352,2048]{1,0:T(8,128)(2,1)} %param.41, bf16[2048,352]{0,1:T(8,128)(2,1)} %param.40, bf16[128,2048]{1,0:T(8,128)(2,1)S(1)} %reshape.561, f32[32,352]{1,0:T(8,128)S(1)} %fusion.41), kind=kOutput, calls=%fused_computation.11 | convolution fusion | flops 92407808 | bytes 3589120 | tf_op jit(solution)/shard_map/dot_general | solution.py:239
  139.3 30.4 %all_to_all.24 = f32[32,4,2048]{2,1,0:T(4,128)S(1)} all-to-all(f32[32,4,2048]{2,1,0:T(4,128)S(1)} %reshape.562), channel_id=1, replica_groups=mesh['seq'=4,'exp'=8] {'seq','exp'}, dimensions={0} | all-to-all | bytes 2097152 | tf_op jit(solution)/shard_map/all_to_all | solution.py:247
  170.1 14.0 %all-gather.7 = bf16[8,4,2048]{2,1,0:T(4,128)(2,1)S(1)} all-gather(bf16[1,4,2048]{2,1,0:T(4,128)(2,1)S(1)} %fusion.54), channel_id=6, replica_groups=mesh['seq'=4,'exp'=8] {'exp'}, dimensions={0}, use_global_device_ids=true | all-gather | bytes 147456 | tf_op jit(solution)/shard_map/all_gather | solution.py:55
  184.1 9.4 %all-gather.5 = bf16[32,4,2048]{2,1,0:T(4,128)(2,1)S(1)} all-gather(bf16[8,4,2048]{2,1,0:T(4,128)(2,1)S(1)} %all-gather.7), channel_id=7, replica_groups=mesh['seq'=4,'exp'=8] {'seq'}, dimensions={0}, use_global_device_ids=true | all-gather | bytes 655360 | tf_op jit(solution)/shard_map/all_gather | solution.py:56
  193.6 4.9 %convolution_reduce_fusion = f32[128]{0:T(128)S(1)} fusion(bf16[128,2048]{1,0:T(8,128)(2,1)S(1)} %reshape.563, bf16[2048,1600]{0,1:T(8,128)(2,1)} %param.43), kind=kOutput, calls=%fused_computation.19 | convolution fusion | flops 839065472 | bytes 7078400 | tf_op jit(solution)/shard_map/dot_general | solution.py:255
  198.5 9.3 %all_to_all.25 = f32[32,1,132]{2,1,0:T(1,128)S(1)} all-to-all(f32[32,1,132]{2,1,0:T(1,128)S(1)} %broadcast_in_dim.151), channel_id=1, replica_groups=mesh['seq'=4,'exp'=8] {'seq','exp'}, dimensions={0} | all-to-all | bytes 33792 | tf_op jit(solution)/shard_map/all_to_all | solution.py:257
  (120 shorter events, 12.3 us)
Async XLA Ops:
  0.6 68.8 %copy-start = (bf16[512,2048]{1,0:T(8,128)(2,1)S(1)}, bf16[512,2048]{1,0:T(8,128)(2,1)}, u32[]{:S(2)}) copy-start(bf16[512,2048]{1,0:T(8,128)(2,1)} %param.31) | copy-start | bytes 6291460
  6.7 8.0 %copy-start.10 = (s32[32]{0:T(128)S(1)}, s32[32]{0:T(128)}, u32[]{:S(2)}) copy-start(s32[32]{0:T(128)} %param.23) | copy-start | bytes 388
  8.4 21.7 %all-to-all-start = ((bf16[8,4,4,2048]{3,2,1,0:T(4,128)(2,1)}), bf16[8,4,4,2048]{3,2,1,0:T(4,128)(2,1)S(1)}, u32[]{:S(2)}, u32[]{:S(2)}) async-start(bf16[8,4,4,2048]{3,2,1,0:T(4,128)(2,1)} %fusion.31), calls=%async_computation | async-start | bytes 1048576 | tf_op jit(solution)/shard_map/all_to_all | solution.py:113
  23.6 4.2 %copy-start.6 = (s32[4,32,6]{1,0,2:T(4,128)S(1)}, s32[4,32,6]{1,0,2:T(4,128)}, u32[]{:S(2)}) copy-start(s32[4,32,6]{1,0,2:T(4,128)} %param.25) | copy-start | bytes 9220
  23.6 16.0 %copy-start.7 = (f32[2048]{0:T(1024)S(1)}, f32[2048]{0:T(1024)}, u32[]{:S(2)}) copy-start(f32[2048]{0:T(1024)} %param.27) | copy-start | bytes 24580
  39.7 2.4 %copy-start.3 = (bf16[512,2048]{1,0:T(8,128)(2,1)S(1)}, bf16[512,2048]{1,0:T(8,128)(2,1)}, u32[]{:S(2)}) copy-start(bf16[512,2048]{1,0:T(8,128)(2,1)} %copy.151) | copy-start | bytes 6291460
  39.7 3.2 %copy-start.2 = (bf16[512,2048]{1,0:T(8,128)(2,1)S(1)}, bf16[512,2048]{1,0:T(8,128)(2,1)}, u32[]{:S(2)}) copy-start(bf16[512,2048]{1,0:T(8,128)(2,1)} %copy.152) | copy-start | bytes 6291460
  60.3 4.1 %collective-permute-start = (f32[1,8320]{1,0:T(1,128)S(1)}, f32[1,8320]{1,0:T(1,128)S(1)}, u32[]{:S(2)}, u32[]{:S(2)}) collective-permute-start(f32[1,8320]{1,0:T(1,128)S(1)} %get-tuple-element.18), channel_id=1, source_target_pairs={{0,8},{8,0},{16,24},{24,16},{1,9},{9,1},{17,25},{25,17},{2,10},{10... | collective-permute-start | bytes 99848 | tf_op jit(solution)/shard_map/ppermute | solution.py:31
  60.8 3.9 %collective-permute-start.1 = (f32[1,8320]{1,0:T(1,128)S(1)}, f32[1,8320]{1,0:T(1,128)S(1)}, u32[]{:S(2)}, u32[]{:S(2)}) collective-permute-start(f32[1,8320]{1,0:T(1,128)S(1)} %get-tuple-element.17), channel_id=1, source_target_pairs={{0,16},{8,24},{16,0},{24,8},{1,17},{9,25},{17,1},{25,9},{2,18},{10... | collective-permute-start | bytes 99848 | tf_op jit(solution)/shard_map/ppermute | solution.py:31
  62.4 4.8 %collective-permute-start.2 = (f32[1,8320]{1,0:T(1,128)S(1)}, f32[1,8320]{1,0:T(1,128)S(1)}, u32[]{:S(2)}, u32[]{:S(2)}) collective-permute-start(f32[1,8320]{1,0:T(1,128)S(1)} %get-tuple-element.16), channel_id=1, source_target_pairs={{0,24},{8,16},{16,8},{24,0},{1,25},{9,17},{17,9},{25,1},{2,26},{10... | collective-permute-start | bytes 99848 | tf_op jit(solution)/shard_map/ppermute | solution.py:31
  68.9 10.1 %copy-start.8 = (f32[2048]{0:T(1024)S(1)}, f32[2048]{0:T(1024)}, u32[]{:S(2)}) copy-start(f32[2048]{0:T(1024)} %param.34) | copy-start | bytes 24580
  70.5 32.7 %copy-start.5 = (bf16[2048,64]{0,1:T(8,128)(2,1)S(1)}, bf16[2048,64]{0,1:T(8,128)(2,1)}, u32[]{:S(2)}) copy-start(bf16[2048,64]{0,1:T(8,128)(2,1)} %param.35) | copy-start | bytes 786436
  70.5 8.4 %all-to-all-start.1 = ((f32[4,4,2048]{2,1,0:T(4,128)}), f32[4,4,2048]{2,1,0:T(4,128)S(1)}, u32[]{:S(2)}, u32[]{:S(2)}) async-start(f32[4,4,2048]{2,1,0:T(4,128)} %fusion.9), calls=%async_computation.1 | async-start | bytes 262144 | tf_op jit(solution)/shard_map/all_to_all | solution.py:205
  134.0 1.4 copy-start.4
  139.3 30.7 %copy-start.9 = (f32[2048]{0:T(1024)S(1)}, f32[2048]{0:T(1024)}, u32[]{:S(2)}) copy-start(f32[2048]{0:T(1024)} %param.42) | copy-start | bytes 24580
  193.6 15.6 %copy-start.1 = (bf16[512,2048]{1,0:T(8,128)(2,1)S(1)}, bf16[512,2048]{1,0:T(8,128)(2,1)}, u32[]{:S(2)}) copy-start(bf16[512,2048]{1,0:T(8,128)(2,1)} %param.31) | copy-start | bytes 6291460
